TPU v7x, 32 devices: a whole 2x2x4 slice. The times are simulated.
32 devices in a mesh: layer: 4 (over y, x), tok: 8 (over z, core).
Axes of the slice: x: 2, y: 2, z: 4, core: 2. Of those that a mesh axis runs over, the one named last changes fastest.
Arguments:
- residual: bfloat16 [4, 1024, 3584], P('layer', 'tok'), may hold values from -6 to 6
- targets: bfloat16 [4, 1024, 3584], P('layer', 'tok'), may hold values from -6 to 6
- block_ids: int32 [4, 1024, 2], P(None, 'tok'), may hold values from 0 to 127, all different within a row; in each aligned block of 128 rows (0 to 127, 128 to 255, ..., all dimensions but the last counted through in order) at most 4 rows name the same one
- encoder_weight: bfloat16 [4, 3584, 16384], P('layer', None, 'tok'), may hold values from -0.09375 to 0.09375
- encoder_bias: float32 [4, 16384], P('layer', 'tok'), may hold values from -3 to 3
- decoder_weight: bfloat16 [4, 4, 16384, 3584], P('layer', None, 'tok'), may hold values from -0.25 to 0.25
- decoder_bias: float32 [4, 3584], P('layer'), may hold values from -3 to 3
Outputs:
- reconstruction: bfloat16 [4, 1024, 3584], P('layer', 'tok')
- error: float32 [4, 1024], P('layer', 'tok')
Inputs may be any that keep to these rules, and one draw needn't show every extreme that they name: `block_ids`: A token's 2 blocks in a layer are distinct. In each layer, the 128 rows of one device (aligned blocks of tokens) name no block more than 4 times, and some block exactly 4 times.
All inputs are finite; a program needn't handle non-finite values.
Results may differ from a plain program's by a relative error of at most 0.0053.
Values may be sent and summed in bfloat16 or wider, within the bound.
No kernel may reach another device: no remote copies, remote signals or barrier semaphores. Data moves between devices by JAX's collectives and lax.ppermute only.
A program may use at most 192 MiB of HBM per device.

v0:
```python
import jax
import jax.numpy as jnp
from jax import lax
from jax.sharding import PartitionSpec as P

BLOCK = 128


def owner_tables(ids_all, owner, per_owner, capacity, tokens):
    layers, _, topk = ids_all.shape
    local = ids_all.reshape(layers, tokens * topk) - owner * per_owner
    owned = (local >= 0) & (local < per_owner)
    onehot = (local[..., None] == jnp.arange(per_owner, dtype=jnp.int32)).astype(jnp.int32)
    rank = jnp.sum((jnp.cumsum(onehot, axis=1) - onehot) * onehot, axis=2)
    slot_count = per_owner * capacity
    slot = jnp.where(owned, local * capacity + rank, slot_count)
    token_of = jnp.arange(tokens * topk, dtype=jnp.int32) // topk
    empty = jnp.full((slot_count,), tokens, jnp.int32)
    return jax.vmap(lambda s: empty.at[s].set(token_of, mode="drop"))(slot)


def body(residual, targets, block_ids, encoder_weight, encoder_bias, decoder_weight, decoder_bias):
    layer_index = lax.axis_index("layer")
    tok_index = lax.axis_index("tok")
    layers = lax.axis_size("layer")
    tok_count = lax.axis_size("tok")
    tok_rows = residual.shape[1]
    width = residual.shape[2]
    topk = block_ids.shape[2]
    per_owner = encoder_weight.shape[2] // BLOCK
    blocks = per_owner * tok_count
    capacity = max(2, 2 * tok_rows * topk // blocks) * tok_count
    slot_count = per_owner * capacity
    tokens = tok_rows * tok_count
    ids_all = lax.all_gather(block_ids, "tok", axis=1, tiled=True)
    table = owner_tables(ids_all, tok_index, per_owner, capacity, tokens)
    res_all = lax.all_gather(residual[0], "tok", axis=0, tiled=True)
    own_table = lax.dynamic_index_in_dim(table, layer_index, 0, keepdims=False)
    rows = jnp.take(res_all, jnp.minimum(own_table, tokens - 1), axis=0)
    enc_blocks = encoder_weight[0].reshape(width, per_owner, BLOCK)
    pre = jnp.einsum(
        "bcd,dbe->bce",
        rows.reshape(per_owner, capacity, width),
        enc_blocks,
        preferred_element_type=jnp.float32,
    )
    pre = pre + encoder_bias[0].reshape(per_owner, 1, BLOCK)
    codes = jnp.maximum(pre, 0.0).astype(jnp.bfloat16)
    all_codes = lax.all_gather(codes, "layer", axis=0, tiled=False)
    terms = jnp.einsum(
        "sbce,sbed->sbcd",
        all_codes,
        decoder_weight[0].reshape(layers, per_owner, BLOCK, width),
        preferred_element_type=jnp.float32,
    ).astype(jnp.bfloat16)
    valid = jnp.arange(layers, dtype=jnp.int32) <= layer_index
    scatter = (table[:, :, None] == jnp.arange(tokens, dtype=jnp.int32)[None, None, :]) & valid[
        :, None, None
    ]
    partial = jnp.einsum(
        "sct,scd->td",
        scatter.astype(jnp.bfloat16),
        terms.reshape(layers, slot_count, width),
        preferred_element_type=jnp.float32,
    )
    summed = lax.psum_scatter(partial.astype(jnp.bfloat16), "tok", scatter_dimension=0, tiled=True)
    recon32 = decoder_bias[0][None, :] + summed.astype(jnp.float32)
    difference = recon32 - targets[0].astype(jnp.float32)
    error = jnp.mean(difference * difference, axis=1)
    return (recon32.astype(jnp.bfloat16)[None], error[None])


def solution(mesh):
    in_specs = (
        P("layer", "tok", None),
        P("layer", "tok", None),
        P(None, "tok", None),
        P("layer", None, "tok"),
        P("layer", "tok"),
        P("layer", None, "tok", None),
        P("layer", None),
    )
    out_specs = (P("layer", "tok", None), P("layer", "tok"))
    return jax.shard_map(body, mesh=mesh, in_specs=in_specs, out_specs=out_specs, check_vma=False)
```

profile of v0, /device:TPU:0, one launch (start us, length us, event | category | flops | bytes accessed | tf_op | source)
XLA Modules:
  0.0 264.9 jit_solution(11410956164858787547)
XLA Ops:
  7.2 0.0 copy-start.3
  7.2 0.0 copy-start.2
  7.2 0.0 all-gather.4.cloned.1.call-start
  7.2 0.7 all-gather.4.cloned.1.call-update
  7.9 0.0 reduce-scatter.2.cloned.1.call-start
  8.0 13.8 %all_gather.12 = s32[4,1024,2]{1,2,0:T(2,128)S(1)} all-gather(s32[4,128,2]{1,2,0:T(2,128)} %param.9), channel_id=1, replica_groups=mesh['layer'=4,'tok'=8] {'tok'}, dimensions={1}, use_global_device_ids=true | all-gather | bytes 36864 | tf_op jit(solution)/shard_map/all_gather | solution.py:35
  21.8 0.6 copy.20
  22.3 0.3 copy.23
  22.7 0.1 fusion.30
  22.7 18.1 %reduce-window.6 = s32[4,16,16,128]{3,2,1,0:T(8,128)S(1)} reduce-window(s32[4,16,16,128]{3,2,1,0:T(8,128)S(1)} %fusion.30, s32[]{:T(128)} %constant.55.clone.1), window={size=1x1x1x128 pad=0_0x0_0x0_0x127_0}, to_apply=%region_0.0 | reduce-window | flops 16646144 | bytes 1048580 | tf_op jit(solution)/shard_map/reduce-window
  40.9 1.3 slice_reduce_fusion
  42.2 0.7 reduce-window.9
  42.9 0.2 broadcast_add_fusion
  43.1 0.1 reduce_window_sum.16
  43.2 0.3 copy.21
  43.6 0.8 copy.18
  44.4 1.6 and.37
  46.0 0.6 copy.19
  46.6 0.3 copy.24
  46.9 0.2 fusion.29
  47.1 0.0 copy-done.3
  47.1 0.1 multiply_reduce_fusion
  47.2 0.0 copy-done.2
  47.2 0.1 and_reduce_fusion
  47.4 30.4 %scatter_custom_fusion = s32[2048]{0:T(1024)S(1)} fusion(s32[8192]{0:T(1024)S(1)} %bitcast.59, s32[8192]{0:T(1024)S(1)} %bitcast.60, s32[]{:T(128)} %constant.30.clone.1), kind=kCustom, calls=%fused_computation.52 | custom fusion | bytes 8196
  77.9 0.1 min.26
  78.0 14.5 %copy.28 = bf16[448,8,16,128]{3,2,1,0:T(8,128)(2,1)} copy(bf16[448,8,16,128]{3,1,2,0:T(8,128)(2,1)} %bitcast.51) | data formatting | bytes 29360128
  92.6 0.0 all-gather.4.cloned.1.call-done
  92.6 0.0 copy-start.4
  92.6 12.0 %gather_fusion = bf16[512,3584]{1,0:T(8,128)(2,1)} fusion(bf16[1024,3584]{1,0:T(8,128)(2,1)} %bitcast.48, s32[1024]{0:T(1024)S(1)} %pad_clamp_fusion), kind=kCustom, calls=%fused_computation | custom fusion | bytes 7342080 | tf_op jit(solution)/shard_map/jit(_take)/gather | solution.py:39
  104.6 0.0 copy-done.4
  104.6 15.1 %fusion.22 = bf16[16,32,128]{2,1,0:T(8,128)(2,1)S(1)} fusion(bf16[3584,16,128]{2,1,0:T(8,128)(2,1)} %bitcast.52, bf16[16,32,3584]{2,1,0:T(8,128)(2,1)} %bitcast.56, pred[16,32]{1,0:T(8,128)(4,1)S(1)} %compare_and_fusion.1, f32[16,128]{1,0:T(8,128)S(1)} %bitcast.62), kind=kOutput, calls=%fused_computation.20 | convolution fusion | flops 471793664 | bytes 18489856 | tf_op jit(solution)/shard_map/bcd,dbe->bce/dot_general | solution.py:41
  119.7 10.4 %all-gather.1 = bf16[64,32,128]{2,1,0:T(8,128)(2,1)S(1)} all-gather(bf16[16,32,128]{2,1,0:T(8,128)(2,1)S(1)} %fusion.22), channel_id=3, replica_groups=mesh['layer'=4,'tok'=8] {'layer'}, dimensions={0}, use_global_device_ids=true | all-gather | bytes 655360 | tf_op jit(solution)/shard_map/all_gather | solution.py:49
  130.1 26.1 %convolution_convert_fusion = bf16[4,16,32,3584]{3,2,1,0:T(8,128)(2,1)} fusion(bf16[4,16,32,128]{3,2,1,0:T(8,128)(2,1)S(1)} %bitcast.57, bf16[4,16,128,3584]{3,2,1,0:T(8,128)(2,1)} %bitcast.49), kind=kOutput, calls=%fused_computation.5 | convolution fusion | flops 1886388224 | bytes 73924608 | tf_op jit(solution)/shard_map/sbce,sbed->sbcd/dot_general | solution.py:50
  156.3 21.6 %bitcast_convert_fusion = bf16[1024,3584]{1,0:T(8,128)(2,1)} fusion(bf16[4,512,3584]{2,1,0:T(8,128)(2,1)} %bitcast.50, s32[4,512]{1,0:T(4,128)S(1)} %reshape.136, pred[4]{0:T(512)(128)(4,1)S(1)} %iota_compare_fusion.3), kind=kOutput, calls=%fused_computation.2 | convolution fusion | flops 15040249856 | bytes 22028292 | tf_op jit(solution)/shard_map/sct,scd->td/dot_general | solution.py:60
  177.9 0.0 copy-start.1
  177.9 0.0 copy-start
  177.9 0.0 reduce-scatter.2.cloned.1.call-update
  177.9 0.7 copy-done.1
  178.6 76.4 %reduce-scatter.2.cloned.1.call-done = bf16[128,3584]{1,0:T(8,128)(2,1)} async-done(((bf16[1024,3584]{1,0:T(8,128)(2,1)}), bf16[128,3584]{1,0:T(8,128)(2,1)}) %reduce-scatter.2.cloned.1.call-update) | async-done | bytes 917520 | tf_op jit(solution)/shard_map/reduce_scatter | solution.py:66
  255.0 0.0 copy-done
  255.0 2.5 fusion.9
  257.5 0.5 multiply_bitcast_fusion
  (16 shorter events, 0.2 us)
Async XLA Ops:
  7.2 40.0 %copy-start.3 = (s32[2]{0:T(128)S(1)}, s32[2]{0:T(128)}, u32[]{:S(2)}) copy-start(s32[2]{0:T(128)} %constant.72) | copy-start | bytes 28
  7.2 40.1 %copy-start.2 = (s32[2]{0:T(128)S(1)}, s32[2]{0:T(128)}, u32[]{:S(2)}) copy-start(s32[2]{0:T(128)} %constant.75) | copy-start | bytes 28
  7.2 85.4 %all-gather.4.cloned.1.call-start = ((), (), s32[]{:S(2)}) async-start(), calls=%async_computation.2 | async-start | bytes 8257536 | tf_op jit(solution)/shard_map/all_gather | solution.py:37
  7.9 247.1 %reduce-scatter.2.cloned.1.call-start = ((), (), s32[]{:S(2)}) async-start(), calls=%async_computation.1 | async-start | bytes 8257536 | tf_op jit(solution)/shard_map/reduce_scatter | solution.py:66
  92.6 12.0 %copy-start.4 = (f32[1,2048]{1,0:T(1,128)S(1)}, f32[1,2048]{1,0:T(1,128)}, u32[]{:S(2)}) copy-start(f32[1,2048]{1,0:T(1,128)} %param.11) | copy-start | bytes 24580
  177.9 0.7 copy-start.1
  177.9 77.1 %copy-start = (bf16[1,128,3584]{2,1,0:T(8,128)(2,1)S(1)}, bf16[1,128,3584]{2,1,0:T(8,128)(2,1)}, u32[]{:S(2)}) copy-start(bf16[1,128,3584]{2,1,0:T(8,128)(2,1)} %param.8) | copy-start | bytes 2752516
Sparse Core Ops, SparseCore 0:
  9.7 76.0 all-gather.3
  178.0 76.9 reduce-scatter.1
where the time goes:
time: 265 us
  waiting for transfers between devices  77.1 us (29%)
  local copies, waits for them, and re-layouts  63.7 us (24%)
  matrix products  62.9 us (24%)
  blocking collectives  24.2 us (9%)
  other arithmetic  22.6 us (9%)
  between operations  14.3 us (5%)
    reduce_scatter x1, waiting for transfers between devices, body(): lax.psum_scatter(partial.astype(jnp.bfloat16), 'tok', scatter_dimension=0...  76.4 us
    unnamed x16, local copies, waits for them, and re-layouts  45.7 us
    dot_general x1, matrix products, body(): jnp.einsum('sbce,sbed->sbcd', all_codes, decoder_weight[0].reshape(layers...  26.1 us
    dot_general x1, matrix products, body(): jnp.einsum('sct,scd->td', scatter.astype(jnp.bfloat16), terms.reshape(lay...  21.6 us
    another operation x3, other arithmetic  19 us
    dot_general x1, matrix products, body(): jnp.einsum('bcd,dbe->bce', rows.reshape(per_owner, capacity, width), enc_...  15.1 us
    all_gather x1, blocking collectives, body(): ids_all = lax.all_gather(block_ids, 'tok', axis=1, tiled=True)  13.8 us
    gather x1, local copies, waits for them, and re-layouts, body(): rows = jnp.take(res_all, jnp.minimum(own_table, tokens - 1), axis=0)  12 us
  transfers between devices with their start and end apart: 2, of which 1 were waited for; matrix products, arithmetic and copies ran while one was open for 27% of the time, Pallas kernels for 0%

commit v1 on v0

--- a/solution.py
+++ b/solution.py
@@ -32,7 +32,26 @@
     capacity = max(2, 2 * tok_rows * topk // blocks) * tok_count
     slot_count = per_owner * capacity
     tokens = tok_rows * tok_count
-    ids_all = lax.all_gather(block_ids, "tok", axis=1, tiled=True)
+    size, index, width_2 = (lax.axis_size("tok"), lax.axis_index("tok"), block_ids.shape[1])
+    ahead = [(i, (i + 1) % size) for i in range(size)]
+    backward = [(i, (i - 1) % size) for i in range(size)]
+    out = jnp.zeros(
+        (*block_ids.shape[:1], size * width_2, *block_ids.shape[1 + 1 :]), block_ids.dtype
+    )
+    out = lax.dynamic_update_slice_in_dim(out, block_ids, index * width_2, axis=1)
+    from_left = from_right = block_ids
+    half = size // 2
+    for step in range(1, half + 1):
+        from_left = lax.ppermute(from_left, "tok", ahead)
+        out = lax.dynamic_update_slice_in_dim(
+            out, from_left, (index - step) % size * width_2, axis=1
+        )
+        if step < size - half:
+            from_right = lax.ppermute(from_right, "tok", backward)
+            out = lax.dynamic_update_slice_in_dim(
+                out, from_right, (index + step) % size * width_2, axis=1
+            )
+    ids_all = out
     table = owner_tables(ids_all, tok_index, per_owner, capacity, tokens)
     res_all = lax.all_gather(residual[0], "tok", axis=0, tiled=True)
     own_table = lax.dynamic_index_in_dim(table, layer_index, 0, keepdims=False)

time: 265 us -> 278 us (1.049)
  blocking collectives: 24.2 us -> 10.5 us
  starting transfers between devices: 0.08 us -> 12 us
  local copies, waits for them, and re-layouts: 63.7 us -> 71.1 us
  other arithmetic: 22.6 us -> 26.1 us
  waiting for transfers between devices: 77.1 us -> 80.6 us
    all_gather x1 -> x0, blocking collectives: 13.8 us -> none  [body(): ids_all = lax.all_gather(block_ids, 'tok', axis=1, tiled=True)]
    ppermute x0 -> x7, starting transfers between devices: none -> 11.9 us  [the longest x3 11.3 us: body(): from_right = lax.ppermute(from_right, 'tok', backward)]
    dynamic_update_slice x0 -> x8, local copies, waits for them, and re-layouts: none -> 5.29 us  [the longest x4 2.65 us: body(): lax.dynamic_update_slice_in_dim(out, from_left, (index - step) % size * w...]
    ppermute x0 -> x7, waiting for transfers between devices: none -> 3.49 us  [the longest x4 3.48 us: body(): from_left = lax.ppermute(from_left, 'tok', ahead)]
    unnamed x16 -> x17, local copies, waits for them, and re-layouts: 45.7 us -> 46.7 us
  transfers between devices with their start and end apart: 2 -> 9, of which waited for: 1 -> 2; matrix products, arithmetic and copies ran while one was open for 27% -> 29% of each run, Pallas kernels for 0% -> 0%
where the time goes in v1:
time: 278 us
  waiting for transfers between devices  80.6 us (29%)
  local copies, waits for them, and re-layouts  71.1 us (26%)
  matrix products  62.9 us (23%)
  other arithmetic  26.1 us (9%)
  between operations  14.4 us (5%)
  starting transfers between devices  12 us (4%)
  blocking collectives  10.5 us (4%)
    reduce_scatter x1, waiting for transfers between devices, body(): lax.psum_scatter(partial.astype(jnp.bfloat16), 'tok', scatter_dimension=0...  76.4 us
    unnamed x17, local copies, waits for them, and re-layouts  46.7 us
    dot_general x1, matrix products, body(): jnp.einsum('sbce,sbed->sbcd', all_codes, decoder_weight[0].reshape(layers...  26.1 us
    dot_general x1, matrix products, body(): jnp.einsum('sct,scd->td', scatter.astype(jnp.bfloat16), terms.reshape(lay...  21.6 us
    another operation x3, other arithmetic  19.8 us
    dot_general x1, matrix products, body(): jnp.einsum('bcd,dbe->bce', rows.reshape(per_owner, capacity, width), enc_...  15.1 us
    gather x1, local copies, waits for them, and re-layouts, body(): rows = jnp.take(res_all, jnp.minimum(own_table, tokens - 1), axis=0)  12.2 us
    ppermute x3, starting transfers between devices, body(): from_right = lax.ppermute(from_right, 'tok', backward)  11.3 us
  transfers between devices with their start and end apart: 9, of which 2 were waited for; matrix products, arithmetic and copies ran while one was open for 29% of the time, Pallas kernels for 0%

profile of v1, /device:TPU:0, one launch (start us, length us, event | category | flops | bytes accessed | tf_op | source)
XLA Modules:
  0.0 277.5 jit_solution(16243504404873140338)
XLA Ops:
  7.2 0.0 all-gather.4.cloned.1.call-start
  7.2 0.7 all-gather.4.cloned.1.call-update
  7.9 0.0 reduce-scatter.2.cloned.1.call-start
  7.9 0.5 collective-permute-start
  8.4 4.1 %collective-permute-start.1 = (s32[4,128,2]{1,2,0:T(2,128)}, s32[4,128,2]{1,2,0:T(2,128)S(1)}, u32[]{:S(2)}, u32[]{:S(2)}) collective-permute-start(s32[4,128,2]{1,2,0:T(2,128)} %param.9), channel_id=1, source_target_pairs={{0,7},{1,0},{2,1},{3,2},{4,3},{5,4},{6,5},{7,6},{8,15},{9,8},{10,9... | collective-permute-start | bytes 12296 | tf_op jit(solution)/shard_map/ppermute | solution.py:50
  12.6 0.9 copy.23
  13.5 1.3 broadcast_in_dim.30
  14.8 0.7 constant_dynamic-update-slice_fusion.7
  15.4 14.7 %copy.39 = bf16[448,8,16,128]{3,2,1,0:T(8,128)(2,1)} copy(bf16[448,8,16,128]{3,1,2,0:T(8,128)(2,1)} %bitcast.55) | data formatting | bytes 29360128
  30.1 0.0 collective-permute-done
  30.1 0.2 copy.24
  30.3 0.1 collective-permute-start.2
  30.3 0.0 collective-permute-done.1
  30.3 0.2 copy.25
  30.5 3.6 %collective-permute-start.3 = (s32[4,128,2]{1,2,0:T(2,128)S(1)}, s32[4,128,2]{1,2,0:T(2,128)S(1)}, u32[]{:S(2)}, u32[]{:S(2)}) collective-permute-start(s32[4,128,2]{1,2,0:T(2,128)S(1)} %collective-permute-done.1), channel_id=1, source_target_pairs={{0,7},{1,0},{2,1},{3,2},{4,3},{5,4},{6,5},{7,6},{8,15},{9,8},{10,9... | collective-permute-start | bytes 12296 | tf_op jit(solution)/shard_map/ppermute | solution.py:50
  34.1 0.7 constant_dynamic-update-slice_fusion.6
  34.7 0.7 constant_dynamic-update-slice_fusion.5
  35.4 0.0 collective-permute-done.2
  35.4 0.2 copy.26
  35.6 0.1 collective-permute-start.4
  35.6 0.0 collective-permute-done.3
  35.6 0.2 copy.27
  35.8 3.6 %collective-permute-start.5 = (s32[4,128,2]{1,2,0:T(2,128)S(1)}, s32[4,128,2]{1,2,0:T(2,128)S(1)}, u32[]{:S(2)}, u32[]{:S(2)}) collective-permute-start(s32[4,128,2]{1,2,0:T(2,128)S(1)} %collective-permute-done.3), channel_id=1, source_target_pairs={{0,7},{1,0},{2,1},{3,2},{4,3},{5,4},{6,5},{7,6},{8,15},{9,8},{10,9... | collective-permute-start | bytes 12296 | tf_op jit(solution)/shard_map/ppermute | solution.py:50
  39.4 0.7 constant_dynamic-update-slice_fusion.4
  40.0 0.7 constant_dynamic-update-slice_fusion.3
  40.7 0.2 copy.28
  40.9 0.1 collective-permute-start.6
  40.9 0.0 collective-permute-done.5
  40.9 0.2 copy.29
  41.1 0.7 constant_dynamic-update-slice_fusion.2
  41.8 0.7 constant_dynamic-update-slice_fusion.1
  42.4 3.5 %collective-permute-done.6 = s32[4,128,2]{1,2,0:T(2,128)S(1)} collective-permute-done((s32[4,128,2]{1,2,0:T(2,128)S(1)}, s32[4,128,2]{1,2,0:T(2,128)S(1)}, u32[]{:S(2)}, u32[]{:S(2)}) %collective-permute-start.6) | collective-permute-done | bytes 4128 | tf_op jit(solution)/shard_map/ppermute | solution.py:45
  45.9 0.2 copy.30
  46.1 0.7 constant_dynamic-update-slice_fusion
  46.7 1.9 broadcast_multiply_fusion
  48.6 0.3 copy.33
  48.9 0.1 fusion.30
  49.0 18.1 %reduce-window.6 = s32[4,16,16,128]{3,2,1,0:T(8,128)S(1)} reduce-window(s32[4,16,16,128]{3,2,1,0:T(8,128)S(1)} %fusion.30, s32[]{:T(128)} %constant.97.clone.1), window={size=1x1x1x128 pad=0_0x0_0x0_0x127_0}, to_apply=%region_0.1 | reduce-window | flops 16646144 | bytes 1048580 | tf_op jit(solution)/shard_map/reduce-window
  67.1 1.3 slice_reduce_fusion
  68.5 0.7 reduce-window.9
  69.1 1.0 broadcast_add_fusion
  70.2 1.2 reduce_window_sum.16
  71.3 0.3 copy.32
  71.6 0.8 compare_and_fusion
  72.5 0.7 reshape.155
  73.1 0.4 copy.36
  73.5 0.3 copy.34
  73.8 0.2 fusion.29
  74.1 0.1 multiply_reduce_fusion
  74.2 0.1 and_reduce_fusion
  74.3 30.4 %scatter_custom_fusion = s32[2048]{0:T(1024)S(1)} fusion(s32[8192]{0:T(1024)S(1)} %bitcast.62, s32[8192]{0:T(1024)S(1)} %bitcast.61, s32[]{:T(128)} %constant.96.clone.1), kind=kCustom, calls=%fused_computation.52 | custom fusion | bytes 8196
  104.8 0.1 min.26
  104.9 0.0 all-gather.4.cloned.1.call-done
  104.9 0.0 copy-start.4
  105.0 12.2 %gather_fusion = bf16[512,3584]{1,0:T(8,128)(2,1)} fusion(bf16[1024,3584]{1,0:T(8,128)(2,1)} %bitcast.50, s32[1024]{0:T(1024)S(1)} %pad_clamp_fusion), kind=kCustom, calls=%fused_computation | custom fusion | bytes 7342080 | tf_op jit(solution)/shard_map/jit(_take)/gather | solution.py:58
  117.1 15.1 %fusion.22 = bf16[16,32,128]{2,1,0:T(8,128)(2,1)S(1)} fusion(bf16[3584,16,128]{2,1,0:T(8,128)(2,1)} %bitcast.56, bf16[16,32,3584]{2,1,0:T(8,128)(2,1)} %bitcast.58, pred[16,32]{1,0:T(8,128)(4,1)S(1)} %compare_and_fusion.1, f32[16,128]{1,0:T(8,128)S(1)} %bitcast.64), kind=kOutput, calls=%fused_computation.21 | convolution fusion | flops 471793664 | bytes 18489856 | tf_op jit(solution)/shard_map/bcd,dbe->bce/dot_general | solution.py:60
  132.3 10.5 %all-gather.1 = bf16[64,32,128]{2,1,0:T(8,128)(2,1)S(1)} all-gather(bf16[16,32,128]{2,1,0:T(8,128)(2,1)S(1)} %fusion.22), channel_id=3, replica_groups=mesh['layer'=4,'tok'=8] {'layer'}, dimensions={0}, use_global_device_ids=true | all-gather | bytes 655360 | tf_op jit(solution)/shard_map/all_gather | solution.py:68
  142.8 26.1 %convolution_convert_fusion = bf16[4,16,32,3584]{3,2,1,0:T(8,128)(2,1)} fusion(bf16[4,16,32,128]{3,2,1,0:T(8,128)(2,1)S(1)} %bitcast.59, bf16[4,16,128,3584]{3,2,1,0:T(8,128)(2,1)} %bitcast.51), kind=kOutput, calls=%fused_computation.5 | convolution fusion | flops 1886388224 | bytes 73924608 | tf_op jit(solution)/shard_map/sbce,sbed->sbcd/dot_general | solution.py:69
  168.9 21.6 %bitcast_convert_fusion = bf16[1024,3584]{1,0:T(8,128)(2,1)} fusion(bf16[4,512,3584]{2,1,0:T(8,128)(2,1)} %bitcast.52, s32[4,512]{1,0:T(4,128)S(1)} %reshape.136, pred[4]{0:T(512)(128)(4,1)S(1)} %iota_compare_fusion.3), kind=kOutput, calls=%fused_computation.2 | convolution fusion | flops 15040249856 | bytes 22028292 | tf_op jit(solution)/shard_map/sct,scd->td/dot_general | solution.py:79
  190.5 0.0 reduce-scatter.2.cloned.1.call-update
  190.5 0.7 copy-done.1
  191.3 76.4 %reduce-scatter.2.cloned.1.call-done = bf16[128,3584]{1,0:T(8,128)(2,1)} async-done(((bf16[1024,3584]{1,0:T(8,128)(2,1)}), bf16[128,3584]{1,0:T(8,128)(2,1)}) %reduce-scatter.2.cloned.1.call-update) | async-done | bytes 917520 | tf_op jit(solution)/shard_map/reduce_scatter | solution.py:85
  267.7 2.5 fusion.9
  270.2 0.5 multiply_bitcast_fusion
  (23 shorter events, 0.2 us)
Async XLA Ops:
  7.2 97.8 %all-gather.4.cloned.1.call-start = ((), (), s32[]{:S(2)}) async-start(), calls=%async_computation.2 | async-start | bytes 8257536 | tf_op jit(solution)/shard_map/all_gather | solution.py:56
  7.9 259.8 %reduce-scatter.2.cloned.1.call-start = ((), (), s32[]{:S(2)}) async-start(), calls=%async_computation.1 | async-start | bytes 8257536 | tf_op jit(solution)/shard_map/reduce_scatter | solution.py:85
  7.9 22.2 %collective-permute-start = (s32[4,128,2]{1,2,0:T(2,128)}, s32[4,128,2]{1,2,0:T(2,128)S(1)}, u32[]{:S(2)}, u32[]{:S(2)}) collective-permute-start(s32[4,128,2]{1,2,0:T(2,128)} %param.9), channel_id=1, source_target_pairs={{0,1},{1,2},{2,3},{3,4},{4,5},{5,6},{6,7},{7,0},{8,9},{9,10},{10,1... | collective-permute-start | bytes 12296 | tf_op jit(solution)/shard_map/ppermute | solution.py:45
  8.4 21.9 %collective-permute-start.1 = (s32[4,128,2]{1,2,0:T(2,128)}, s32[4,128,2]{1,2,0:T(2,128)S(1)}, u32[]{:S(2)}, u32[]{:S(2)}) collective-permute-start(s32[4,128,2]{1,2,0:T(2,128)} %param.9), channel_id=1, source_target_pairs={{0,7},{1,0},{2,1},{3,2},{4,3},{5,4},{6,5},{7,6},{8,15},{9,8},{10,9... | collective-permute-start | bytes 12296 | tf_op jit(solution)/shard_map/ppermute | solution.py:50
  30.3 5.1 %collective-permute-start.2 = (s32[4,128,2]{1,2,0:T(2,128)S(1)}, s32[4,128,2]{1,2,0:T(2,128)S(1)}, u32[]{:S(2)}, u32[]{:S(2)}) collective-permute-start(s32[4,128,2]{1,2,0:T(2,128)S(1)} %collective-permute-done), channel_id=1, source_target_pairs={{0,1},{1,2},{2,3},{3,4},{4,5},{5,6},{6,7},{7,0},{8,9},{9,10},{10,1... | collective-permute-start | bytes 12296 | tf_op jit(solution)/shard_map/ppermute | solution.py:45
  30.5 5.1 %collective-permute-start.3 = (s32[4,128,2]{1,2,0:T(2,128)S(1)}, s32[4,128,2]{1,2,0:T(2,128)S(1)}, u32[]{:S(2)}, u32[]{:S(2)}) collective-permute-start(s32[4,128,2]{1,2,0:T(2,128)S(1)} %collective-permute-done.1), channel_id=1, source_target_pairs={{0,7},{1,0},{2,1},{3,2},{4,3},{5,4},{6,5},{7,6},{8,15},{9,8},{10,9... | collective-permute-start | bytes 12296 | tf_op jit(solution)/shard_map/ppermute | solution.py:50
  35.6 5.1 %collective-permute-start.4 = (s32[4,128,2]{1,2,0:T(2,128)S(1)}, s32[4,128,2]{1,2,0:T(2,128)S(1)}, u32[]{:S(2)}, u32[]{:S(2)}) collective-permute-start(s32[4,128,2]{1,2,0:T(2,128)S(1)} %collective-permute-done.2), channel_id=1, source_target_pairs={{0,1},{1,2},{2,3},{3,4},{4,5},{5,6},{6,7},{7,0},{8,9},{9,10},{10,1... | collective-permute-start | bytes 12296 | tf_op jit(solution)/shard_map/ppermute | solution.py:45
  35.8 5.1 %collective-permute-start.5 = (s32[4,128,2]{1,2,0:T(2,128)S(1)}, s32[4,128,2]{1,2,0:T(2,128)S(1)}, u32[]{:S(2)}, u32[]{:S(2)}) collective-permute-start(s32[4,128,2]{1,2,0:T(2,128)S(1)} %collective-permute-done.3), channel_id=1, source_target_pairs={{0,7},{1,0},{2,1},{3,2},{4,3},{5,4},{6,5},{7,6},{8,15},{9,8},{10,9... | collective-permute-start | bytes 12296 | tf_op jit(solution)/shard_map/ppermute | solution.py:50
  40.9 5.0 %collective-permute-start.6 = (s32[4,128,2]{1,2,0:T(2,128)S(1)}, s32[4,128,2]{1,2,0:T(2,128)S(1)}, u32[]{:S(2)}, u32[]{:S(2)}) collective-permute-start(s32[4,128,2]{1,2,0:T(2,128)S(1)} %collective-permute-done.4), channel_id=1, source_target_pairs={{0,1},{1,2},{2,3},{3,4},{4,5},{5,6},{6,7},{7,0},{8,9},{9,10},{10,1... | collective-permute-start | bytes 12296 | tf_op jit(solution)/shard_map/ppermute | solution.py:45
  41.8 32.3 %copy-start.3 = (s32[2]{0:T(128)S(1)}, s32[2]{0:T(128)}, u32[]{:S(2)}) copy-start(s32[2]{0:T(128)} %constant.124) | copy-start | bytes 28
  42.4 31.7 %copy-start.2 = (s32[2]{0:T(128)S(1)}, s32[2]{0:T(128)}, u32[]{:S(2)}) copy-start(s32[2]{0:T(128)} %constant.127) | copy-start | bytes 28
  104.9 12.2 %copy-start.4 = (f32[1,2048]{1,0:T(1,128)S(1)}, f32[1,2048]{1,0:T(1,128)}, u32[]{:S(2)}) copy-start(f32[1,2048]{1,0:T(1,128)} %param.11) | copy-start | bytes 24580
  190.5 0.7 copy-start.1
  190.5 77.2 %copy-start = (bf16[1,128,3584]{2,1,0:T(8,128)(2,1)S(1)}, bf16[1,128,3584]{2,1,0:T(8,128)(2,1)}, u32[]{:S(2)}) copy-start(bf16[1,128,3584]{2,1,0:T(8,128)(2,1)} %param.8) | copy-start | bytes 2752516
Sparse Core Ops, SparseCore 0:
  9.6 76.3 all-gather.3
  190.7 76.9 reduce-scatter.1
